TPU v7x, 256 devices: a whole 4x4x8 slice. The times are simulated.
256 devices in a mesh: joint: 8 (over z), frame: 32 (over y, x, core).
Axes of the slice: x: 4, y: 4, z: 8, core: 2. Of those that a mesh axis runs over, the one named last changes fastest.
Arguments:
- tokens: bfloat16 [64, 768, 1536], P('joint', 'frame'), may hold values from -500 to 500
- norm_gain: float32 [1536], replicated, may hold values from 0.1 to 1.9
- qkv_weight: bfloat16 [1536, 3072], P('frame'), may hold values from -3 to 3
- out_grad: bfloat16 [64, 768, 1024], P('joint', 'frame'), may hold values from -6 to 6
Outputs:
- attended: bfloat16 [64, 768, 1024], P('joint', 'frame')
- token_grad: bfloat16 [64, 768, 1536], P('joint', 'frame')
- weight_grad: float32 [1536, 3072], P('frame')
- gain_grad: float32 [1536], replicated
All inputs are finite; a program needn't handle non-finite values.
Results may differ from a plain program's by a relative error of at most 0.029.
The roundings to bfloat16 on the way count: a program that leaves them out, or rounds other values in their place, can miss the bound.
Values may be sent and summed in bfloat16 or wider, within the bound.
No kernel may reach another device: no remote copies, remote signals or barrier semaphores. Data moves between devices by JAX's collectives and lax.ppermute only.
A program may use at most 128 MiB of HBM per device.

v0:
```python
import math
import jax
import jax.numpy as jnp
from jax import lax
from jax.sharding import PartitionSpec as P

HEADS = 8
HDIM = 128
EPSILON = 1e-05


def attention_local(queries, keys_all, values_all, upstream, inv_root, groups):
    scores = (
        jnp.einsum("fihd,fjhd->fhij", queries, keys_all, preferred_element_type=jnp.float32)
        * inv_root
    )
    probs = jax.nn.softmax(scores, axis=-1)
    probs_low = probs.astype(jnp.bfloat16)
    attended = jnp.einsum(
        "fhij,fjhd->fihd", probs_low, values_all, preferred_element_type=jnp.float32
    ).astype(jnp.bfloat16)
    prob_grad = jnp.einsum(
        "fihd,fjhd->fhij", upstream, values_all, preferred_element_type=jnp.float32
    )
    carried = jnp.sum(probs * prob_grad, axis=-1, keepdims=True)
    score_grad = (probs * (prob_grad - carried) * inv_root).astype(jnp.bfloat16)
    query_grad = jnp.einsum(
        "fhij,fjhd->fihd", score_grad, keys_all, preferred_element_type=jnp.float32
    ).astype(jnp.bfloat16)
    frames, joints = (queries.shape[0], queries.shape[1])
    size = joints // groups
    sg = score_grad.reshape(frames, HEADS, groups, size, joints)
    pl_ = probs_low.reshape(frames, HEADS, groups, size, joints)
    qg = queries.reshape(frames, groups, size, HEADS, HDIM)
    ug = upstream.reshape(frames, groups, size, HEADS, HDIM)
    key_part = jnp.einsum("fhgij,fgihd->fgjhd", sg, qg, preferred_element_type=jnp.float32)
    value_part = jnp.einsum("fhgij,fgihd->fgjhd", pl_, ug, preferred_element_type=jnp.float32)
    key_grad = jnp.sum(key_part.astype(jnp.bfloat16).astype(jnp.float32), axis=1).astype(
        jnp.bfloat16
    )
    value_grad = jnp.sum(value_part.astype(jnp.bfloat16).astype(jnp.float32), axis=1).astype(
        jnp.bfloat16
    )
    return (attended, query_grad, key_grad, value_grad)


def per_device(tokens, norm_gain, qkv_weight, out_grad):
    joint_rows, frame_rows, width = tokens.shape
    inner = out_grad.shape[2]
    joint_count = lax.axis_size("joint")
    total_tokens = joint_rows * frame_rows * joint_count * lax.axis_size("frame")
    grad_scale = 1.0 / math.sqrt(total_tokens)
    inv_root = 1.0 / math.sqrt(HDIM)
    joints = joint_rows * joint_count
    local_frames = frame_rows // joint_count
    count = joints * local_frames
    whole = lax.all_gather(qkv_weight, "frame", axis=0, tiled=True)
    packed = jnp.concatenate([tokens, out_grad], axis=2)
    packed = lax.all_to_all(packed, "joint", 1, 0, tiled=True)
    packed = packed.transpose(1, 0, 2)
    flat = packed[:, :, :width].reshape(count, width).astype(jnp.float32)
    upstream = packed[:, :, width:].reshape(local_frames, joints, HEADS, HDIM)
    rinv = lax.rsqrt(jnp.mean(flat * flat, axis=1, keepdims=True) + EPSILON)
    normed = flat * rinv
    scaled = (normed * norm_gain).astype(jnp.bfloat16)
    projected = jnp.dot(scaled, whole, preferred_element_type=jnp.float32).astype(jnp.bfloat16)
    projected = projected.reshape(local_frames, joints, 3, HEADS, HDIM)
    queries = projected[:, :, 0]
    keys_all = projected[:, :, 1]
    values_all = projected[:, :, 2]
    attended, query_grad, key_grad, value_grad = attention_local(
        queries, keys_all, values_all, upstream, inv_root, joint_count
    )
    qkv_grad = jnp.concatenate(
        [
            query_grad.reshape(count, inner),
            key_grad.reshape(count, inner),
            value_grad.reshape(count, inner),
        ],
        axis=1,
    )
    product = lax.dot_general(
        scaled, qkv_grad, (((0,), (0,)), ((), ())), preferred_element_type=jnp.float32
    )
    frame_sum = lax.psum_scatter(
        (product * grad_scale).astype(jnp.bfloat16), "frame", scatter_dimension=0, tiled=True
    )
    joint_part = lax.psum_scatter(frame_sum, "joint", scatter_dimension=1, tiled=True)
    weight_grad = lax.all_gather(joint_part, "joint", axis=1, tiled=True).astype(jnp.float32)
    normed_grad = lax.dot_general(
        qkv_grad, whole, (((1,), (1,)), ((), ())), preferred_element_type=jnp.float32
    )
    gain_part = jnp.sum(normed_grad * normed, axis=0) * grad_scale
    gain_grad = lax.psum(gain_part, ("joint", "frame"))
    upper = normed_grad * norm_gain
    token_grad = rinv * (upper - normed * jnp.mean(upper * normed, axis=1, keepdims=True))
    token_grad = token_grad.astype(jnp.bfloat16).reshape(local_frames, joints, width)
    back = jnp.concatenate(
        [attended.reshape(local_frames, joints, inner), token_grad], axis=2
    ).transpose(1, 0, 2)
    back = lax.all_to_all(back, "joint", 0, 1, tiled=True)
    attended_out = back[:, :, :inner]
    token_out = back[:, :, inner:]
    return (attended_out, token_out, weight_grad, gain_grad)


def solution(mesh):
    placed = (P("joint", "frame", None), P(), P("frame", None), P("joint", "frame", None))
    return jax.shard_map(
        per_device,
        mesh=mesh,
        in_specs=placed,
        out_specs=(P("joint", "frame", None), P("joint", "frame", None), P("frame", None), P()),
        check_vma=False,
    )
```

profile of v0, /device:TPU:32, one launch (start us, length us, event | category | flops | bytes accessed | tf_op | source)
XLA Modules:
  0.0 318.2 jit_solution(16296569881700968422)
XLA Ops:
  7.2 0.7 all-gather.2.cloned.1.call-update
  8.0 1.2 copy.77
  9.2 0.2 copy.76
  9.4 0.1 pad_maximum_fusion
  9.4 34.2 %all_to_all.36 = bf16[8,24,2560]{2,0,1:T(8,128)(2,1)S(1)} all-to-all(bf16[8,24,2560]{2,0,1:T(8,128)(2,1)S(1)} %pad_maximum_fusion), channel_id=1, replica_groups=mesh['joint'=8,'frame'=32] {'joint'}, dimensions={1} | all-to-all | bytes 1966080 | tf_op jit(solution)/shard_map/all_to_all | solution.py:59
  43.7 0.1 copy.151
  43.8 0.2 multiply_reduce_fusion.2
  44.0 0.1 rsqrt.12
  44.1 0.1 slice_convert_fusion
  44.2 0.1 bitcast_multiply_fusion
  44.4 28.9 %all-gather.2.cloned.1.call-done = bf16[1536,3072]{1,0:T(8,128)(2,1)} async-done(((bf16[48,3072]{1,0:T(8,128)(2,1)}), bf16[1536,3072]{1,0:T(8,128)(2,1)}) %all-gather.2.cloned.1.call-update) | async-done | bytes 9437200 | tf_op jit(solution)/shard_map/all_gather | solution.py:57
  73.3 5.7 %fusion.3 = bf16[24,8,24,128]{3,1,2,0:T(8,128)(2,1)S(1)} fusion(bf16[1536,3072]{1,0:T(8,128)(2,1)} %all-gather.2.cloned.1.call-done, f32[192,1536]{1,0:T(8,128)S(1)} %bitcast_multiply_fusion, f32[1536]{0:T(1024)S(1)} %copy-done.9), kind=kOutput, calls=%fused_computation.7 | convolution fusion | flops 1813118976 | bytes 11802624 | tf_op jit(solution)/shard_map/dot_general | solution.py:66
  79.0 0.2 copy.111
  79.2 1.1 fusion.27
  80.3 0.3 fusion.12
  80.7 2.4 fusion.28
  83.1 2.7 fusion.10
  85.8 2.4 fusion.8
  88.2 0.1 fusion.26
  88.3 0.9 copy.91
  89.2 2.1 convert_reduce_fusion
  91.4 0.3 copy.93
  91.6 0.9 copy.87
  92.6 2.1 convert_reduce_fusion.1
  94.7 0.3 copy.90
  95.0 0.3 copy.86
  95.4 1.0 copy-done.8
  96.5 0.4 copy-done.1
  96.9 5.1 %multiply_convert_fusion = bf16[1536,3072]{1,0:T(8,128)(2,1)} fusion(bf16[192,3072]{1,0:T(8,128)(2,1)S(1)} %bitcast_dynamic-update-slice_fusion, f32[192,1536]{1,0:T(8,128)S(1)} %copy-done.1, f32[1536]{0:T(1024)S(1)} %copy-done.9), kind=kOutput, calls=%fused_computation.2 | convolution fusion | flops 1821966336 | bytes 11802624 | tf_op jit(solution)/shard_map/dot_general | solution.py:82
  102.0 0.3 fusion.9
  102.3 0.3 copy.102
  102.6 0.1 reshape.73
  102.7 0.9 copy-done.2
  103.6 7.4 %multiply_reduce_fusion = (f32[1536]{0:T(1024)S(1)}, f32[192]{0:T(256)S(1)}, f32[192,1536]{1,0:T(8,128)S(1)}) fusion(f32[192,1536]{1,0:T(8,128)S(1)} %copy-done.2, f32[1536]{0:T(1024)S(1)} %copy-done.9, bf16[192,3072]{1,0:T(8,128)(2,1)} %copy-done.8, bf16[1536,3072]{1,0:T(8,128)(2,1)} %all-gather.2.cloned.1.call-done), kind=kOutput, calls=%fused_computation.20 | convolution fusion | flops 1813412096 | bytes 12989184 | tf_op jit(solution)/shard_map/dot_general | solution.py:90
  111.0 0.3 multiply_convert_fusion.1
  111.3 0.5 copy.95
  111.8 1.7 maximum_bitcast_fusion
  113.5 7.5 %all-to-all-start.1 = ((bf16[64,3,2560]{2,1,0:T(4,128)(2,1)}), bf16[64,3,2560]{2,1,0:T(4,128)(2,1)S(1)}, u32[]{:S(2)}, u32[]{:S(2)}) async-start(bf16[64,3,2560]{2,1,0:T(4,128)(2,1)} %maximum_bitcast_fusion), calls=%async_computation.1 | async-start | bytes 2621440 | tf_op jit(solution)/shard_map/all_to_all | solution.py:101
  121.0 84.0 %reduce-scatter.5.cloned.1.call-done = bf16[48,3072]{1,0:T(8,128)(2,1)} async-done(((bf16[1536,3072]{1,0:T(8,128)(2,1)}), bf16[48,3072]{1,0:T(8,128)(2,1)}) %reduce-scatter.5.cloned.1.call-update) | async-done | bytes 294928 | tf_op jit(solution)/shard_map/reduce_scatter | solution.py:85
  204.9 2.2 copy.103
  207.1 75.9 %psum.7 = f32[1536]{0:T(1024)} all-reduce(f32[1536]{0:T(1024)S(1)} %broadcast_multiply_fusion), channel_id=1, replica_groups=mesh['joint'=8,'frame'=32] {'joint','frame'}, use_global_device_ids=true, to_apply=%region_10.0 | all-reduce | flops 1536 | bytes 12288 | tf_op jit(solution)/shard_map/psum | solution.py:94
  283.1 0.2 copy.150
  283.3 0.1 copy.97
  283.5 1.0 copy.99
  284.5 1.0 copy.98
  285.4 1.0 copy.104
  286.4 24.4 %all_gather.7 = bf16[48,3072]{1,0:T(8,128)(2,1)S(1)} all-gather(bf16[48,384]{1,0:T(8,128)(2,1)S(1)} %copy.104), channel_id=1, replica_groups=mesh['joint'=8,'frame'=32] {'joint'}, dimensions={1}, use_global_device_ids=true | all-gather | bytes 331776 | tf_op jit(solution)/shard_map/all_gather | solution.py:89
  310.8 0.9 convert_element_type.69
  (32 shorter events, 0.4 us)
Async XLA Ops:
  7.2 2.0 copy-start.4
  7.2 66.1 %all-gather.2.cloned.1.call-start = ((), (), s32[]{:S(2)}) async-start(), calls=%async_computation.4 | async-start | bytes 9732096 | tf_op jit(solution)/shard_map/all_gather | solution.py:57
  7.9 197.0 %reduce-scatter.5.cloned.1.call-start = ((), (), s32[]{:S(2)}) async-start(), calls=%async_computation.5 | async-start | bytes 9732096 | tf_op jit(solution)/shard_map/reduce_scatter | solution.py:85
  44.2 29.1 %copy-start.9 = (f32[1536]{0:T(1024)S(1)}, f32[1536]{0:T(1024)}, u32[]{:S(2)}) copy-start(f32[1536]{0:T(1024)} %param.5) | copy-start | bytes 18436
  44.4 34.6 %copy-start = (f32[192,1536]{1,0:T(8,128)}, f32[192,1536]{1,0:T(8,128)S(1)}, u32[]{:S(2)}) copy-start(f32[192,1536]{1,0:T(8,128)S(1)} %bitcast_multiply_fusion) | copy-start | bytes 3538948
  85.8 2.4 copy-start.3
  89.2 2.4 copy-start.7
  91.3 1.2 copy-start.5
  92.6 2.4 copy-start.6
  95.2 1.7 copy-start.1
  95.4 1.0 copy-start.8
  102.3 1.3 copy-start.2
  113.5 169.6 %all-to-all-start.1 = ((bf16[64,3,2560]{2,1,0:T(4,128)(2,1)}), bf16[64,3,2560]{2,1,0:T(4,128)(2,1)S(1)}, u32[]{:S(2)}, u32[]{:S(2)}) async-start(bf16[64,3,2560]{2,1,0:T(4,128)(2,1)} %maximum_bitcast_fusion), calls=%async_computation.1 | async-start | bytes 2621440 | tf_op jit(solution)/shard_map/all_to_all | solution.py:101
  121.0 164.5 %reduce-scatter.7.cloned.1.call-start = ((), (), s32[]{:S(2)}) async-start(), calls=%async_computation.6 | async-start | bytes 884736
Sparse Core Ops, SparseCore 0:
  10.5 62.7 all-gather.1
  102.1 102.7 reduce-scatter.4
  207.5 36.8 reduce-scatter.6
where the time goes:
time: 319 us; the launch traced here: 318 us
  blocking collectives  135 us (42%)
  waiting for transfers between devices  114 us (36%)
  matrix products  28.2 us (9%)
  local copies, waits for them, and re-layouts  14.4 us (5%)
  between operations  14 us (4%)
  starting transfers between devices  7.55 us (2%)
  other arithmetic  5.87 us (2%)
    reduce_scatter x1, waiting for transfers between devices, per_device(): lax.psum_scatter((product * grad_scale).astype(jnp.bfloat16), 'frame', sc...  84 us
    psum x1, blocking collectives, per_device(): gain_grad = lax.psum(gain_part, ('joint', 'frame'))  75.9 us
    all_to_all x1, blocking collectives, per_device(): packed = lax.all_to_all(packed, 'joint', 1, 0, tiled=True)  34.2 us
    all_gather x1, waiting for transfers between devices, per_device(): whole = lax.all_gather(qkv_weight, 'frame', axis=0, tiled=True)  28.9 us
    all_gather x1, blocking collectives, per_device(): lax.all_gather(joint_part, 'joint', axis=1, tiled=True).astype(jnp.float32)  24.4 us
    unnamed x29, local copies, waits for them, and re-layouts  9.18 us
    all_to_all x1, starting transfers between devices, per_device(): back = lax.all_to_all(back, 'joint', 0, 1, tiled=True)  7.47 us
    dot_general x1, matrix products, per_device(): lax.dot_general(qkv_grad, whole, (((1,), (1,)), ((), ())), preferred_elem...  7.44 us
  transfers between devices with their start and end apart: 4, of which 2 were waited for; matrix products, arithmetic and copies ran while one was open for 5% of the time, Pallas kernels for 0%

commit v1 on v0

--- a/solution.py
+++ b/solution.py
@@ -91,7 +91,8 @@
         qkv_grad, whole, (((1,), (1,)), ((), ())), preferred_element_type=jnp.float32
     )
     gain_part = jnp.sum(normed_grad * normed, axis=0) * grad_scale
-    gain_grad = lax.psum(gain_part, ("joint", "frame"))
+    shards = lax.all_gather(gain_part, ("joint", "frame"))
+    gain_grad = jnp.sum(shards, axis=0)
     upper = normed_grad * norm_gain
     token_grad = rinv * (upper - normed * jnp.mean(upper * normed, axis=1, keepdims=True))
     token_grad = token_grad.astype(jnp.bfloat16).reshape(local_frames, joints, width)

time: 319 us -> 383 us (1.20)
  waiting for transfers between devices: 114 us -> 250 us
  blocking collectives: 135 us -> 59.1 us
  other arithmetic: 5.87 us -> 10.3 us
    all_gather x0 -> x1, waiting for transfers between devices: none -> 102 us  [per_device(): shards = lax.all_gather(gain_part, ('joint', 'frame'))]
    psum x1 -> x0, blocking collectives: 75.9 us -> none  [per_device(): gain_grad = lax.psum(gain_part, ('joint', 'frame'))]
    unnamed x4 -> x5, waiting for transfers between devices: 0.72 us -> 37 us
    unnamed x29 -> x28, local copies, waits for them, and re-layouts: 9.18 us -> 9.4 us
  transfers between devices with their start and end apart: 4 -> 5, of which waited for: 2 -> 4; matrix products, arithmetic and copies ran while one was open for 5% -> 6% of each run, Pallas kernels for 0% -> 0%
where the time goes in v1:
time: 383 us; the launch traced here: 382 us
  waiting for transfers between devices  250 us (65%)
  blocking collectives  59.1 us (15%)
  matrix products  27.4 us (7%)
  between operations  14.1 us (4%)
  local copies, waits for them, and re-layouts  13.3 us (3%)
  other arithmetic  10.3 us (3%)
  starting transfers between devices  7.78 us (2%)
    all_gather x1, waiting for transfers between devices, per_device(): shards = lax.all_gather(gain_part, ('joint', 'frame'))  102 us
    reduce_scatter x1, waiting for transfers between devices, per_device(): lax.psum_scatter((product * grad_scale).astype(jnp.bfloat16), 'frame', sc...  82.5 us
    unnamed x5, waiting for transfers between devices  37 us
    all_to_all x1, blocking collectives, per_device(): packed = lax.all_to_all(packed, 'joint', 1, 0, tiled=True)  34.2 us
    all_gather x1, waiting for transfers between devices, per_device(): whole = lax.all_gather(qkv_weight, 'frame', axis=0, tiled=True)  28 us
    all_gather x1, blocking collectives, per_device(): lax.all_gather(joint_part, 'joint', axis=1, tiled=True).astype(jnp.float32)  24.8 us
    unnamed x28, local copies, waits for them, and re-layouts  9.4 us
    dot_general x1, matrix products, per_device(): lax.dot_general(qkv_grad, whole, (((1,), (1,)), ((), ())), preferred_elem...  8.38 us
  transfers between devices with their start and end apart: 5, of which 4 were waited for; matrix products, arithmetic and copies ran while one was open for 6% of the time, Pallas kernels for 0%

profile of v1, /device:TPU:32, one launch (start us, length us, event | category | flops | bytes accessed | tf_op | source)
XLA Modules:
  0.0 381.5 jit_solution(14124280932670015126)
XLA Ops:
  7.2 0.7 all-gather.5.cloned.1.call-update
  8.0 1.2 copy.77
  9.2 0.2 copy.76
  9.4 34.2 %all_to_all.36 = bf16[8,24,2560]{2,0,1:T(8,128)(2,1)S(1)} all-to-all(bf16[8,24,2560]{2,0,1:T(8,128)(2,1)S(1)} %pad_maximum_fusion), channel_id=1, replica_groups=mesh['joint'=8,'frame'=32] {'joint'}, dimensions={1} | all-to-all | bytes 1966080 | tf_op jit(solution)/shard_map/all_to_all | solution.py:59
  43.8 0.2 multiply_reduce_fusion.2
  44.0 0.1 slice_convert_fusion
  44.2 1.1 bitcast_multiply_fusion
  45.3 28.0 %all-gather.5.cloned.1.call-done = bf16[1536,3072]{1,0:T(8,128)(2,1)} async-done(((bf16[48,3072]{1,0:T(8,128)(2,1)}), bf16[1536,3072]{1,0:T(8,128)(2,1)}) %all-gather.5.cloned.1.call-update) | async-done | bytes 9437200 | tf_op jit(solution)/shard_map/all_gather | solution.py:57
  73.3 6.1 %fusion.3 = bf16[24,8,24,128]{3,1,2,0:T(8,128)(2,1)S(1)} fusion(bf16[1536,3072]{1,0:T(8,128)(2,1)} %all-gather.5.cloned.1.call-done, f32[192,1536]{1,0:T(8,128)} %bitcast_multiply_fusion, f32[1536]{0:T(1024)S(1)} %copy-done.8), kind=kOutput, calls=%fused_computation.7 | convolution fusion | flops 1813118976 | bytes 11802624 | tf_op jit(solution)/shard_map/dot_general | solution.py:66
  79.4 0.2 copy.111
  79.6 0.2 fusion.27
  79.8 1.2 fusion.12
  81.1 1.3 fusion.28
  82.3 3.0 fusion.10
  85.4 2.9 fusion.8
  88.3 0.1 fusion.26
  88.4 0.2 copy.91
  88.6 1.0 convert_reduce_fusion
  89.6 0.3 copy.93
  89.9 1.2 copy.87
  91.1 1.0 convert_reduce_fusion.1
  92.2 0.3 copy.90
  92.5 0.3 copy.86
  92.9 1.0 copy-done.7
  94.0 0.4 copy-done
  94.4 5.1 %multiply_convert_fusion = bf16[1536,3072]{1,0:T(8,128)(2,1)} fusion(bf16[192,3072]{1,0:T(8,128)(2,1)S(1)} %bitcast_dynamic-update-slice_fusion, f32[192,1536]{1,0:T(8,128)S(1)} %copy-done, f32[1536]{0:T(1024)S(1)} %copy-done.8), kind=kOutput, calls=%fused_computation.2 | convolution fusion | flops 1821966336 | bytes 11802624 | tf_op jit(solution)/shard_map/dot_general | solution.py:82
  99.5 0.2 all-gather.7.cloned.1.call-start
  99.7 8.4 %multiply_reduce_fusion = (f32[1536]{0:T(1024)S(1)}, f32[192]{0:T(256)S(1)}, f32[192,1536]{1,0:T(8,128)}) fusion(f32[192,1536]{1,0:T(8,128)S(1)} %copy-done, f32[1536]{0:T(1024)S(1)} %copy-done.8, bf16[192,3072]{1,0:T(8,128)(2,1)} %copy-done.7, bf16[1536,3072]{1,0:T(8,128)(2,1)} %all-gather.5.cloned.1.call-done), kind=kOutput, calls=%fused_computation.20 | convolution fusion | flops 1813412096 | bytes 12989184 | tf_op jit(solution)/shard_map/dot_general | solution.py:90
  108.1 0.6 reshape.83
  108.7 0.3 fusion.9
  109.1 0.3 copy.102
  109.3 0.1 reshape.86
  109.4 0.6 copy-done.1
  110.0 0.3 multiply_convert_fusion.1
  110.3 0.5 copy.95
  110.8 1.7 maximum_bitcast_fusion
  112.5 7.5 %all-to-all-start.1 = ((bf16[64,3,2560]{2,1,0:T(4,128)(2,1)}), bf16[64,3,2560]{2,1,0:T(4,128)(2,1)S(1)}, u32[]{:S(2)}, u32[]{:S(2)}) async-start(bf16[64,3,2560]{2,1,0:T(4,128)(2,1)} %maximum_bitcast_fusion), calls=%async_computation.1 | async-start | bytes 2621440 | tf_op jit(solution)/shard_map/all_to_all | solution.py:102
  119.9 82.5 %reduce-scatter.5.cloned.1.call-done = bf16[48,3072]{1,0:T(8,128)(2,1)} async-done(((bf16[1536,3072]{1,0:T(8,128)(2,1)}), bf16[48,3072]{1,0:T(8,128)(2,1)}) %reduce-scatter.5.cloned.1.call-update) | async-done | bytes 294928 | tf_op jit(solution)/shard_map/reduce_scatter | solution.py:85
  202.4 2.1 copy.103
  204.6 0.2 copy.150
  205.0 1.0 copy.99
  206.0 1.0 copy.98
  206.9 102.2 %all-gather.7.cloned.1.call-done = f32[256,1,1536]{2,1,0:T(1,128)} async-done(((f32[1,1,1536]{2,1,0:T(1,128)}), f32[256,1,1536]{2,1,0:T(1,128)}) %all-gather.7.cloned.1.call-update) | async-done | bytes 1572880 | tf_op jit(solution)/shard_map/all_gather | solution.py:94
  309.1 2.9 reduce_sum.91
  312.0 36.3 %reduce-scatter.7.cloned.1.call-done = bf16[384,48]{1,0:T(8,128)(2,1)} async-done(((bf16[3072,48]{1,0:T(8,128)(2,1)}), bf16[384,48]{1,0:T(8,128)(2,1)}) %reduce-scatter.7.cloned.1.call-update) | async-done | bytes 36880
  348.3 1.0 copy.104
  349.3 24.8 %all_gather.11 = bf16[48,3072]{1,0:T(8,128)(2,1)S(1)} all-gather(bf16[48,384]{1,0:T(8,128)(2,1)S(1)} %copy.104), channel_id=1, replica_groups=mesh['joint'=8,'frame'=32] {'joint'}, dimensions={1}, use_global_device_ids=true | all-gather | bytes 331776 | tf_op jit(solution)/shard_map/all_gather | solution.py:89
  374.1 0.9 convert_element_type.69
  (34 shorter events, 0.7 us)
Async XLA Ops:
  7.2 2.0 copy-start.3
  7.2 66.1 %all-gather.5.cloned.1.call-start = ((), (), s32[]{:S(2)}) async-start(), calls=%async_computation.4 | async-start | bytes 9732096 | tf_op jit(solution)/shard_map/all_gather | solution.py:57
  7.9 194.5 %reduce-scatter.5.cloned.1.call-start = ((), (), s32[]{:S(2)}) async-start(), calls=%async_computation.5 | async-start | bytes 9732096 | tf_op jit(solution)/shard_map/reduce_scatter | solution.py:85
  44.2 29.1 %copy-start.8 = (f32[1536]{0:T(1024)S(1)}, f32[1536]{0:T(1024)}, u32[]{:S(2)}) copy-start(f32[1536]{0:T(1024)} %param.5) | copy-start | bytes 18436
  79.8 2.5 copy-start.4
  85.4 2.9 copy-start.2
  89.6 1.5 copy-start.5
  91.1 1.3 copy-start.6
  92.7 1.7 copy-start
  92.9 1.0 copy-start.7
  99.5 209.6 %all-gather.7.cloned.1.call-start = ((), (), s32[]{:S(2)}) async-start(), calls=%async_computation.6 | async-start | bytes 1579008 | tf_op jit(solution)/shard_map/all_gather | solution.py:94
  108.7 1.3 copy-start.1
  112.5 92.1 %all-to-all-start.1 = ((bf16[64,3,2560]{2,1,0:T(4,128)(2,1)}), bf16[64,3,2560]{2,1,0:T(4,128)(2,1)S(1)}, u32[]{:S(2)}, u32[]{:S(2)}) async-start(bf16[64,3,2560]{2,1,0:T(4,128)(2,1)} %maximum_bitcast_fusion), calls=%async_computation.1 | async-start | bytes 2621440 | tf_op jit(solution)/shard_map/all_to_all | solution.py:102
  119.9 228.4 %reduce-scatter.7.cloned.1.call-start = ((), (), s32[]{:S(2)}) async-start(), calls=%async_computation.7 | async-start | bytes 884736
Sparse Core Ops, SparseCore 0:
  10.5 62.7 all-gather.4
  99.6 102.7 reduce-scatter.4
  206.7 102.3 all-gather.6
  311.5 36.7 reduce-scatter.6
